TPU v7x, 128 devices: a whole 4x4x4 slice. The times are simulated.
128 devices in a mesh: sect: 4 (over y), blk: 32 (over x, z, core).
Axes of the slice: x: 4, y: 4, z: 4, core: 2. Of those that a mesh axis runs over, the one named last changes fastest.
Arguments:
- theta: bfloat16 [4, 4096, 2048], P('sect', 'blk'), may hold values from -6 to 6
- left_env: bfloat16 [4, 8, 4096, 4096], P('sect', None, 'blk'), may hold values from -0.125 to 0.125
- sector_ids: int32 [4, 4096], P('sect'), may hold values from 0 to 15, never falling along the last dimension, each value on 1 to 2560 neighbouring positions
- local_ops: float32 [4, 8, 16, 16], P('sect'), may hold values from -0.5 to 0.5
- edge_env: float32 [128, 128], replicated, may hold values from -0.5 to 0.5
Outputs:
- updated: bfloat16 [4, 4096, 2048], P('sect', 'blk')
- outgoing: float32 [4, 128, 128], P('sect')
Inputs may be any that keep to these rules, and one draw needn't show every extreme that they name: `sector_ids`: within each section the sector numbers never fall along the rows; each sector holds 1 to 2560 rows and one holds exactly 2560.
All inputs are finite; a program needn't handle non-finite values.
Results may differ from a plain program's by a relative error of at most 0.00165.
Values may be sent and summed in bfloat16 or wider, within the bound.
No kernel may reach another device: no remote copies, remote signals or barrier semaphores. Data moves between devices by JAX's collectives and lax.ppermute only.
A program may use at most 128 MiB of HBM per device.

v0:
```python
import jax
import jax.numpy as jnp
from jax import lax
from jax.sharding import PartitionSpec as P


def shifted(array, axis, by):
    peers = lax.axis_size(axis)
    pairs = [(i, i + by) for i in range(peers) if 0 <= i + by < peers]
    return lax.ppermute(array, axis, pairs)


def matprod(first, second):
    return jnp.dot(first, second, precision=lax.Precision.HIGHEST)


def per_device(theta, left_env, sector_ids, local_ops, edge_env):
    rows_dev = theta.shape[1]
    width = theta.shape[2]
    chain_w = left_env.shape[1]
    phys = local_ops.shape[2]
    cols = width // phys
    theta_loc = theta[0]
    env_loc = left_env[0]
    sec_all = sector_ids[0]
    ops_loc = local_ops[0]
    my_block = lax.axis_index("blk")
    row_start = my_block * rows_dev
    my_sec = lax.dynamic_slice_in_dim(sec_all, row_start, rows_dev, 0)
    same = my_sec[:, None] == sec_all[None, :]
    masked = jnp.where(same[None, :, :], env_loc, jnp.zeros_like(env_loc))
    applied = jnp.einsum(
        "wij,jx->wix",
        masked,
        lax.all_gather(theta_loc, "blk", axis=0, tiled=True),
        preferred_element_type=jnp.float32,
    )
    applied = applied.reshape(chain_w, rows_dev, phys, cols)
    acted = jnp.einsum("wpq,wiqc->ipc", ops_loc, applied, precision=lax.Precision.HIGHEST)
    theta_f = theta_loc.astype(jnp.float32).reshape(rows_dev, phys, cols)
    partial_intersection = jnp.einsum(
        "ipc,ipd->cd", theta_f, acted, precision=lax.Precision.HIGHEST
    )
    intersection = lax.psum(partial_intersection, "blk")
    transfer = (
        intersection
        * jnp.sqrt(jnp.float32(cols))
        / jnp.sqrt(jnp.sum(intersection * intersection) + 1e-06)
    )
    sect_no = lax.axis_index("sect")
    incoming = edge_env
    for step_no in range(lax.axis_size("sect") - 1):
        leaving = matprod(incoming, transfer)
        passed = shifted(leaving, "sect", 1)
        incoming = jnp.where(sect_no == 0, edge_env, passed)
    outgoing = matprod(incoming, transfer)
    result = jnp.einsum("ipc,cd->ipd", acted, incoming, precision=lax.Precision.HIGHEST)
    updated = result.reshape(1, rows_dev, width).astype(jnp.bfloat16)
    return (updated, outgoing[None])


def solution(mesh):
    placed = (
        P("sect", "blk", None),
        P("sect", None, "blk", None),
        P("sect", None),
        P("sect", None, None, None),
        P(),
    )
    return jax.shard_map(
        per_device,
        mesh=mesh,
        in_specs=placed,
        out_specs=(P("sect", "blk", None), P("sect", None, None)),
        check_vma=False,
    )
```

profile of v0, /device:TPU:8, one launch (start us, length us, event | category | flops | bytes accessed | tf_op | source)
XLA Modules:
  0.0 271.1 jit_solution(17785318184022447140)
XLA Ops:
  7.2 0.7 all-gather.3.cloned.1.call-update
  7.9 0.0 all-reduce.2.cloned.1.call-start
  8.0 1.1 copy.21
  9.1 0.7 dynamic-slice_bitcast_fusion
  9.8 1.1 broadcast_compare_fusion
  10.9 74.4 %all-gather.3.cloned.1.call-done = bf16[1,4096,2048]{2,1,0:T(8,128)(2,1)} async-done(((bf16[1,128,2048]{2,1,0:T(8,128)(2,1)}), bf16[1,4096,2048]{2,1,0:T(8,128)(2,1)}) %all-gather.3.cloned.1.call-update) | async-done | bytes 16777232 | tf_op jit(solution)/shard_map/all_gather | solution.py:35
  85.2 15.1 %copy.20 = bf16[512,8,16,128]{3,2,1,0:T(8,128)(2,1)} copy(bf16[512,8,16,128]{3,1,2,0:T(8,128)(2,1)} %bitcast.44) | data formatting | bytes 33554432
  100.3 25.4 %fusion = f32[8,128,16,128]{3,1,2,0:T(8,128)} fusion(bf16[16,128,4096,1]{1,0,2,3:T(8,128)(2,1)} %bitcast.45, bf16[1,8,128,4096]{3,2,1,0:T(8,128)(2,1)} %param.6, pred[128,4096]{1,0:T(8,128)(4,1)S(1)} %broadcast_compare_fusion), kind=kOutput, calls=%fused_computation | convolution fusion | flops 17184063488 | bytes 34078720 | tf_op jit(solution)/shard_map/wij,jx->wix/dot_general | solution.py:32
  125.8 12.4 %fusion.8 = f32[128,16,128]{2,1,0:T(8,128)S(1)} fusion(f32[8,128,16,128]{3,1,2,0:T(8,128)} %fusion, f32[1,8,16,16]{3,2,1,0:T(8,128)S(1)} %copy-done), kind=kOutput, calls=%fused_computation.8 | convolution fusion | flops 402653184 | bytes 9445376 | tf_op jit(solution)/shard_map/wpq,wiqc->ipc/dot_general | solution.py:39
  138.2 1.6 convolution_bitcast_fusion
  139.8 96.2 %all-reduce.2.cloned.1.call-done = f32[128,128]{0,1:T(8,128)} async-done(((f32[128,128]{0,1:T(8,128)}), f32[128,128]{0,1:T(8,128)}) %all-reduce.2.cloned.1.call-update) | async-done | bytes 65552 | tf_op jit(solution)/shard_map/psum | solution.py:44
  236.1 1.5 multiply_reduce_fusion
  238.2 1.1 convolution_bitcast_fusion.2
  239.3 3.4 %collective-permute-start = (f32[128,128]{1,0:T(8,128)S(1)}, f32[128,128]{1,0:T(8,128)S(1)}, u32[]{:S(2)}, u32[]{:S(2)}) collective-permute-start(f32[128,128]{1,0:T(8,128)S(1)} %convolution_bitcast_fusion.2), channel_id=1, source_target_pairs={{0,32},{32,64},{64,96},{1,33},{33,65},{65,97},{2,34},{34,66},{66,9... | collective-permute-start | bytes 196616 | tf_op jit(solution)/shard_map/ppermute | solution.py:10
  242.7 2.8 %collective-permute-done = f32[128,128]{1,0:T(8,128)S(1)} collective-permute-done((f32[128,128]{1,0:T(8,128)S(1)}, f32[128,128]{1,0:T(8,128)S(1)}, u32[]{:S(2)}, u32[]{:S(2)}) %collective-permute-start) | collective-permute-done | bytes 65568 | tf_op jit(solution)/shard_map/ppermute | solution.py:10
  245.6 1.1 fusion.16
  246.7 3.4 %collective-permute-start.1 = (f32[128,128]{1,0:T(8,128)S(1)}, f32[128,128]{1,0:T(8,128)S(1)}, u32[]{:S(2)}, u32[]{:S(2)}) collective-permute-start(f32[128,128]{1,0:T(8,128)S(1)} %fusion.16), channel_id=1, source_target_pairs={{0,32},{32,64},{64,96},{1,33},{33,65},{65,97},{2,34},{34,66},{66,9... | collective-permute-start | bytes 196616 | tf_op jit(solution)/shard_map/ppermute | solution.py:10
  250.1 2.8 %collective-permute-done.1 = f32[128,128]{1,0:T(8,128)S(1)} collective-permute-done((f32[128,128]{1,0:T(8,128)S(1)}, f32[128,128]{1,0:T(8,128)S(1)}, u32[]{:S(2)}, u32[]{:S(2)}) %collective-permute-start.1) | collective-permute-done | bytes 65568 | tf_op jit(solution)/shard_map/ppermute | solution.py:10
  252.8 1.1 fusion.14
  253.9 3.4 %collective-permute-start.2 = (f32[128,128]{1,0:T(8,128)S(1)}, f32[128,128]{1,0:T(8,128)S(1)}, u32[]{:S(2)}, u32[]{:S(2)}) collective-permute-start(f32[128,128]{1,0:T(8,128)S(1)} %fusion.14), channel_id=1, source_target_pairs={{0,32},{32,64},{64,96},{1,33},{33,65},{65,97},{2,34},{34,66},{66,9... | collective-permute-start | bytes 196616 | tf_op jit(solution)/shard_map/ppermute | solution.py:10
  257.3 2.8 %collective-permute-done.2 = f32[128,128]{1,0:T(8,128)S(1)} collective-permute-done((f32[128,128]{1,0:T(8,128)S(1)}, f32[128,128]{1,0:T(8,128)S(1)}, u32[]{:S(2)}, u32[]{:S(2)}) %collective-permute-start.2) | collective-permute-done | bytes 65568 | tf_op jit(solution)/shard_map/ppermute | solution.py:10
  260.1 1.4 convolution_convert_fusion
  261.5 1.0 copy.11
  262.5 1.7 convolution_bitcast_fusion.1
  (6 shorter events, 0.1 us)
Async XLA Ops:
  7.2 118.6 %copy-start = (f32[1,8,16,16]{3,2,1,0:T(8,128)S(1)}, f32[1,8,16,16]{3,2,1,0:T(8,128)}, u32[]{:S(2)}) copy-start(f32[1,8,16,16]{3,2,1,0:T(8,128)} %param.8) | copy-start | bytes 24580
  7.2 78.1 %all-gather.3.cloned.1.call-start = ((), (), s32[]{:S(2)}) async-start(), calls=%async_computation.1 | async-start | bytes 17301504 | tf_op jit(solution)/shard_map/all_gather | solution.py:35
  7.9 228.1 %all-reduce.2.cloned.1.call-start = ((), (), s32[]{:S(2)}) async-start(), calls=%async_computation | async-start | bytes 131072 | tf_op jit(solution)/shard_map/psum | solution.py:44
  125.8 112.5 %copy-start.1 = (f32[128,128]{1,0:T(8,128)S(1)}, f32[128,128]{1,0:T(8,128)}, u32[]{:S(2)}) copy-start(f32[128,128]{1,0:T(8,128)} %param.9) | copy-start | bytes 196612
  239.3 6.2 %collective-permute-start = (f32[128,128]{1,0:T(8,128)S(1)}, f32[128,128]{1,0:T(8,128)S(1)}, u32[]{:S(2)}, u32[]{:S(2)}) collective-permute-start(f32[128,128]{1,0:T(8,128)S(1)} %convolution_bitcast_fusion.2), channel_id=1, source_target_pairs={{0,32},{32,64},{64,96},{1,33},{33,65},{65,97},{2,34},{34,66},{66,9... | collective-permute-start | bytes 196616 | tf_op jit(solution)/shard_map/ppermute | solution.py:10
  246.7 6.2 %collective-permute-start.1 = (f32[128,128]{1,0:T(8,128)S(1)}, f32[128,128]{1,0:T(8,128)S(1)}, u32[]{:S(2)}, u32[]{:S(2)}) collective-permute-start(f32[128,128]{1,0:T(8,128)S(1)} %fusion.16), channel_id=1, source_target_pairs={{0,32},{32,64},{64,96},{1,33},{33,65},{65,97},{2,34},{34,66},{66,9... | collective-permute-start | bytes 196616 | tf_op jit(solution)/shard_map/ppermute | solution.py:10
  253.9 6.2 %collective-permute-start.2 = (f32[128,128]{1,0:T(8,128)S(1)}, f32[128,128]{1,0:T(8,128)S(1)}, u32[]{:S(2)}, u32[]{:S(2)}) collective-permute-start(f32[128,128]{1,0:T(8,128)S(1)} %fusion.14), channel_id=1, source_target_pairs={{0,32},{32,64},{64,96},{1,33},{33,65},{65,97},{2,34},{34,66},{66,9... | collective-permute-start | bytes 196616 | tf_op jit(solution)/shard_map/ppermute | solution.py:10
Sparse Core Ops, SparseCore 0:
  10.2 74.9 all-gather.2
  139.9 96.0 all-reduce.1
where the time goes:
time: 272 us; the launch traced here: 271 us
  waiting for transfers between devices  180 us (66%)
  matrix products  45.9 us (17%)
  local copies, waits for them, and re-layouts  17.9 us (7%)
  between operations  14.8 us (5%)
  starting transfers between devices  10.2 us (4%)
    psum x1, waiting for transfers between devices, per_device(): intersection = lax.psum(partial_intersection, 'blk')  96.2 us
    all_gather x1, waiting for transfers between devices, per_device(): lax.all_gather(theta_loc, 'blk', axis=0, tiled=True)  74.4 us
    dot_general x1, matrix products, per_device(): jnp.einsum('wij,jx->wix', masked, lax.all_gather(theta_loc, 'blk', axis=0...  25.4 us
    unnamed x7, local copies, waits for them, and re-layouts  17.2 us
    dot_general x1, matrix products, per_device(): jnp.einsum('wpq,wiqc->ipc', ops_loc, applied, precision=lax.Precision.HIG...  12.4 us
    ppermute x3, starting transfers between devices, shifted(): return lax.ppermute(array, axis, pairs)  10.2 us
    ppermute x3, waiting for transfers between devices, shifted(): return lax.ppermute(array, axis, pairs)  8.33 us
  transfers between devices with their start and end apart: 5, of which 5 were waited for; matrix products, arithmetic and copies ran while one was open for 1% of the time, Pallas kernels for 0%

commit v1 on v0

--- a/solution.py
+++ b/solution.py
@@ -2,6 +2,7 @@
 import jax.numpy as jnp
 from jax import lax
 from jax.sharding import PartitionSpec as P
+from jax.lax import all_to_all, axis_size
 
 
 def shifted(array, axis, by):
@@ -29,10 +30,18 @@
     my_sec = lax.dynamic_slice_in_dim(sec_all, row_start, rows_dev, 0)
     same = my_sec[:, None] == sec_all[None, :]
     masked = jnp.where(same[None, :, :], env_loc, jnp.zeros_like(env_loc))
+
+    def watch_the_shards(body, dev_axis):
+        n_peers_all = axis_size(dev_axis)
+        items = [n_peers_all if num == 0 else 1 for num in range(body.ndim)]
+        return all_to_all(
+            jnp.tile(body, items), concat_axis=0, split_axis=0, axis_name=dev_axis, tiled=True
+        )
+
     applied = jnp.einsum(
         "wij,jx->wix",
         masked,
-        lax.all_gather(theta_loc, "blk", axis=0, tiled=True),
+        watch_the_shards(theta_loc, "blk"),
         preferred_element_type=jnp.float32,
     )
     applied = applied.reshape(chain_w, rows_dev, phys, cols)

time: 272 us -> 478 us (1.76)
  waiting for transfers between devices: 180 us -> 374 us
  starting transfers between devices: 10.2 us -> 18.6 us
  local copies, waits for them, and re-layouts: 17.9 us -> 23 us
    all_to_all x0 -> x1, waiting for transfers between devices: none -> 240 us  [watch_the_shards(): all_to_all(jnp.tile(body, items), concat_axis=0, split_axis=0, axis_name=...]
    all_gather x1 -> x0, waiting for transfers between devices: 74.4 us -> none  [per_device(): lax.all_gather(theta_loc, 'blk', axis=0, tiled=True)]
    psum x1, waiting for transfers between devices: 96.2 us -> 126 us  [per_device(): intersection = lax.psum(partial_intersection, 'blk')]
    all_to_all x0 -> x1, starting transfers between devices: none -> 8.42 us  [watch_the_shards(): all_to_all(jnp.tile(body, items), concat_axis=0, split_axis=0, axis_name=...]
    another operation x0 -> x1, local copies, waits for them, and re-layouts: none -> 6.82 us  [watch_the_shards(): jnp.tile(body, items)]
    unnamed x7 -> x11, local copies, waits for them, and re-layouts: 17.2 us -> 16.2 us
  transfers between devices with their start and end apart: 5 -> 5, of which waited for: 5 -> 5; matrix products, arithmetic and copies ran while one was open for 1% -> 0% of each run, Pallas kernels for 0% -> 0%
where the time goes in v1:
time: 478 us
  waiting for transfers between devices  374 us (78%)
  matrix products  45.9 us (10%)
  local copies, waits for them, and re-layouts  23 us (5%)
  starting transfers between devices  18.6 us (4%)
  between operations  14.8 us (3%)
    all_to_all x1, waiting for transfers between devices, watch_the_shards(): all_to_all(jnp.tile(body, items), concat_axis=0, split_axis=0, axis_name=...  240 us
    psum x1, waiting for transfers between devices, per_device(): intersection = lax.psum(partial_intersection, 'blk')  126 us
    dot_general x1, matrix products, per_device(): jnp.einsum('wij,jx->wix', masked, watch_the_shards(theta_loc, 'blk'), pre...  25.4 us
    unnamed x11, local copies, waits for them, and re-layouts  16.2 us
    dot_general x1, matrix products, per_device(): jnp.einsum('wpq,wiqc->ipc', ops_loc, applied, precision=lax.Precision.HIG...  12.4 us
    ppermute x3, starting transfers between devices, shifted(): return lax.ppermute(array, axis, pairs)  10.2 us
  transfers between devices with their start and end apart: 5, of which 5 were waited for; matrix products, arithmetic and copies ran while one was open for 0% of the time, Pallas kernels for 0%

profile of v1, /device:TPU:8, one launch (start us, length us, event | category | flops | bytes accessed | tf_op | source)
XLA Modules:
  0.0 477.8 jit_solution(15257883737034673962)
XLA Ops:
  7.2 6.8 %tile.9 = bf16[32,128,2048]{2,1,0:T(8,128)(2,1)} broadcast(bf16[128,2048]{1,0:T(8,128)(2,1)} %bitcast.46), dimensions={1,2} | broadcast | bytes 17301504 | tf_op jit(solution)/shard_map/tile | solution.py:38
  14.0 8.4 %all-to-all-start = ((bf16[32,128,2048]{2,1,0:T(8,128)(2,1)}), bf16[32,128,2048]{2,1,0:T(8,128)(2,1)}, u32[]{:S(2)}, u32[]{:S(2)}) async-start(bf16[32,128,2048]{2,1,0:T(8,128)(2,1)} %tile.9), calls=%async_computation | async-start | bytes 33554432 | tf_op jit(solution)/shard_map/all_to_all | solution.py:37
  22.4 0.0 all-reduce.2.cloned.1.call-start
  22.5 0.1 copy.21
  22.6 0.4 broadcast_compare_fusion
  23.0 239.6 %all-to-all-done = bf16[32,128,2048]{2,1,0:T(8,128)(2,1)} async-done(((bf16[32,128,2048]{2,1,0:T(8,128)(2,1)}), bf16[32,128,2048]{2,1,0:T(8,128)(2,1)}, u32[]{:S(2)}, u32[]{:S(2)}) %all-to-all-start) | async-done | bytes 16777248 | tf_op jit(solution)/shard_map/all_to_all | solution.py:37
  262.6 15.1 %copy.20 = bf16[512,8,16,128]{3,2,1,0:T(8,128)(2,1)} copy(bf16[512,8,16,128]{3,1,2,0:T(8,128)(2,1)} %bitcast.24) | data formatting | bytes 33554432
  277.7 25.4 %fusion = f32[8,128,16,128]{3,1,2,0:T(8,128)} fusion(bf16[16,128,4096,1]{1,0,2,3:T(8,128)(2,1)} %bitcast.45, bf16[1,8,128,4096]{3,2,1,0:T(8,128)(2,1)} %param.6, pred[128,4096]{1,0:T(8,128)(4,1)S(1)} %broadcast_compare_fusion), kind=kOutput, calls=%fused_computation | convolution fusion | flops 17184063488 | bytes 34078720 | tf_op jit(solution)/shard_map/wij,jx->wix/dot_general | solution.py:41
  303.1 12.4 %fusion.8 = f32[128,16,128]{2,1,0:T(8,128)S(1)} fusion(f32[8,128,16,128]{3,1,2,0:T(8,128)} %fusion, f32[1,8,16,16]{3,2,1,0:T(8,128)S(1)} %copy-done), kind=kOutput, calls=%fused_computation.8 | convolution fusion | flops 402653184 | bytes 9445376 | tf_op jit(solution)/shard_map/wpq,wiqc->ipc/dot_general | solution.py:48
  315.5 1.6 convolution_bitcast_fusion
  317.2 125.6 %all-reduce.2.cloned.1.call-done = f32[128,128]{0,1:T(8,128)} async-done(((f32[128,128]{0,1:T(8,128)}), f32[128,128]{0,1:T(8,128)}) %all-reduce.2.cloned.1.call-update) | async-done | bytes 65552 | tf_op jit(solution)/shard_map/psum | solution.py:53
  442.8 1.5 multiply_reduce_fusion
  444.9 1.1 convolution_bitcast_fusion.2
  446.1 3.4 collective-permute-start
  449.5 2.8 collective-permute-done
  452.3 1.1 fusion.16
  453.4 3.4 collective-permute-start.1
  456.8 2.8 collective-permute-done.1
  459.5 1.1 fusion.14
  460.7 3.4 collective-permute-start.2
  464.1 2.8 collective-permute-done.2
  466.8 1.4 convolution_convert_fusion
  468.2 1.0 copy.11
  469.2 1.7 convolution_bitcast_fusion.1
  (10 shorter events, 0.0 us)
Async XLA Ops:
  7.2 296.0 %copy-start = (f32[1,8,16,16]{3,2,1,0:T(8,128)S(1)}, f32[1,8,16,16]{3,2,1,0:T(8,128)}, u32[]{:S(2)}) copy-start(f32[1,8,16,16]{3,2,1,0:T(8,128)} %param.8) | copy-start | bytes 24580
  14.0 8.5 %copy-start.1 = (bf16[1,128,2048]{2,1,0:T(8,128)(2,1)S(1)}, bf16[1,128,2048]{2,1,0:T(8,128)(2,1)}, u32[]{:S(2)}) copy-start(bf16[1,128,2048]{2,1,0:T(8,128)(2,1)} %param.5) | copy-start | bytes 1572868
  14.0 8.6 %copy-start.3 = (s32[1,4096]{1,0:T(1,128)S(1)}, s32[1,4096]{1,0:T(1,128)}, u32[]{:S(2)}) copy-start(s32[1,4096]{1,0:T(1,128)} %param.7) | copy-start | bytes 49156
  14.0 248.6 %all-to-all-start = ((bf16[32,128,2048]{2,1,0:T(8,128)(2,1)}), bf16[32,128,2048]{2,1,0:T(8,128)(2,1)}, u32[]{:S(2)}, u32[]{:S(2)}) async-start(bf16[32,128,2048]{2,1,0:T(8,128)(2,1)} %tile.9), calls=%async_computation | async-start | bytes 33554432 | tf_op jit(solution)/shard_map/all_to_all | solution.py:37
  22.4 420.4 %all-reduce.2.cloned.1.call-start = ((), (), s32[]{:S(2)}) async-start(), calls=%async_computation.1 | async-start | bytes 131072 | tf_op jit(solution)/shard_map/psum | solution.py:53
  303.1 141.8 %copy-start.2 = (f32[128,128]{1,0:T(8,128)S(1)}, f32[128,128]{1,0:T(8,128)}, u32[]{:S(2)}) copy-start(f32[128,128]{1,0:T(8,128)} %param.9) | copy-start | bytes 196612
  446.1 6.2 %collective-permute-start = (f32[128,128]{1,0:T(8,128)S(1)}, f32[128,128]{1,0:T(8,128)S(1)}, u32[]{:S(2)}, u32[]{:S(2)}) collective-permute-start(f32[128,128]{1,0:T(8,128)S(1)} %convolution_bitcast_fusion.2), channel_id=1, source_target_pairs={{0,32},{32,64},{64,96},{1,33},{33,65},{65,97},{2,34},{34,66},{66,9... | collective-permute-start | bytes 196616 | tf_op jit(solution)/shard_map/ppermute | solution.py:11
  453.4 6.2 %collective-permute-start.1 = (f32[128,128]{1,0:T(8,128)S(1)}, f32[128,128]{1,0:T(8,128)S(1)}, u32[]{:S(2)}, u32[]{:S(2)}) collective-permute-start(f32[128,128]{1,0:T(8,128)S(1)} %fusion.16), channel_id=1, source_target_pairs={{0,32},{32,64},{64,96},{1,33},{33,65},{65,97},{2,34},{34,66},{66,9... | collective-permute-start | bytes 196616 | tf_op jit(solution)/shard_map/ppermute | solution.py:11
  460.7 6.2 %collective-permute-start.2 = (f32[128,128]{1,0:T(8,128)S(1)}, f32[128,128]{1,0:T(8,128)S(1)}, u32[]{:S(2)}, u32[]{:S(2)}) collective-permute-start(f32[128,128]{1,0:T(8,128)S(1)} %fusion.14), channel_id=1, source_target_pairs={{0,32},{32,64},{64,96},{1,33},{33,65},{65,97},{2,34},{34,66},{66,9... | collective-permute-start | bytes 196616 | tf_op jit(solution)/shard_map/ppermute | solution.py:11
Sparse Core Ops, SparseCore 0:
  317.3 125.4 all-reduce.1
